TPU v7x, 512 devices: a whole 4x8x8 slice. The times are simulated.
512 devices in a mesh: depth: 32 (over y, x), lat: 16 (over z, core).
Axes of the slice: x: 4, y: 8, z: 8, core: 2. Of those that a mesh axis runs over, the one named last changes fastest.
Arguments:
- thermal_state: float32 [1024, 8, 2048], P('depth', None, 'lat'), may hold values from -5 to 5
- sideways_face_flux_factor: float32 [1024, 8, 2048], P('depth', None, 'lat'), may hold values from 1 to 10
- downward_face_flux_factor: float32 [1024, 8, 2048], P('depth', None, 'lat'), may hold values from 1 to 10
Outputs:
- final_temperature: float32 [1024, 8, 2048], P('depth', None, 'lat')
All inputs are finite; a program needn't handle non-finite values.
Results may differ from a plain program's by a relative error of at most 0.0013.
Values sent between devices are 32-bit elements; how exact they have to be, the bound alone decides.
No kernel may reach another device: no remote copies, remote signals or barrier semaphores. Data moves between devices by JAX's collectives and lax.ppermute only.
A program may use at most 64 MiB of HBM per device.

v0:
```python
import jax
import jax.numpy as jnp
from jax import lax
from jax.sharding import PartitionSpec as P

sideways_coupling_quotient = 20.0
ratio_z = 2000.0


def extended(x, sides, width):
    for axis, dim in sides:
        count, length = (lax.axis_size(axis), x.shape[dim])
        up = [(i, (i + 1) % count) for i in range(count - 1)]
        down = [(j, i) for i, j in up]
        last = lax.slice_in_dim(x, length - width, length, axis=dim)
        first = lax.slice_in_dim(x, 0, width, axis=dim)
        before = lax.ppermute(last, axis, up)
        after = lax.ppermute(first, axis, down)
        x = jnp.concatenate([before, x, after], axis=dim)
    return x


def from_behind(x, axis, by):
    count = lax.axis_size(axis)
    pairs = [(i, i + by) for i in range(count) if 0 <= i + by < count]
    return lax.ppermute(x, axis, pairs)


def take_rows(values, start, stop, axis_index):
    return lax.slice_in_dim(values, start, stop, axis=axis_index)


def moved(values, stride, axis_index, filler, forward):
    count = values.shape[axis_index]
    pad_shape = list(values.shape)
    pad_shape[axis_index] = stride
    padding = jnp.full(pad_shape, filler, values.dtype)
    if forward:
        return jnp.concatenate(
            [take_rows(values, stride, count, axis_index), padding], axis=axis_index
        )
    return jnp.concatenate(
        [padding, take_rows(values, 0, count - stride, axis_index)], axis=axis_index
    )


def level_update(lower_band, diagonal, upper_band, rights, below, above):
    alpha_term = -lower_band / below[1]
    gamma_term = -upper_band / above[1]
    new_diagonal = diagonal + alpha_term * below[2] + gamma_term * above[0]
    new_rights = tuple(
        (
            column + alpha_term * low_col + gamma_term * high_col
            for column, low_col, high_col in zip(rights, below[3], above[3])
        )
    )
    return (alpha_term * below[0], new_diagonal, gamma_term * above[2], new_rights)


def cyclic(lower_band, diagonal, upper_band, rights, axis_index):
    count = lower_band.shape[axis_index]
    stride = 1
    while stride < count:
        below = (
            moved(lower_band, stride, axis_index, 0.0, False),
            moved(diagonal, stride, axis_index, 1.0, False),
            moved(upper_band, stride, axis_index, 0.0, False),
            tuple((moved(column, stride, axis_index, 0.0, False) for column in rights)),
        )
        above = (
            moved(lower_band, stride, axis_index, 0.0, True),
            moved(diagonal, stride, axis_index, 1.0, True),
            moved(upper_band, stride, axis_index, 0.0, True),
            tuple((moved(column, stride, axis_index, 0.0, True) for column in rights)),
        )
        lower_band, diagonal, upper_band, rights = level_update(
            lower_band, diagonal, upper_band, rights, below, above
        )
        stride = stride * 2
    return tuple((column / diagonal for column in rights))


def partition_solve(lower_band, upper_inner, rights, axis_index, fetch_next, reduced, fetch_prev):
    count = lower_band.shape[axis_index]
    inner_lower = take_rows(lower_band, 0, count - 1, axis_index)
    diagonal = 1.0 - inner_lower - upper_inner
    positions = lax.broadcasted_iota(jnp.int32, inner_lower.shape, axis_index)
    first_lower = take_rows(inner_lower, 0, 1, axis_index)
    last_upper = take_rows(upper_inner, count - 2, count - 1, axis_index)
    solve_lower = jnp.where(positions == 0, 0.0, inner_lower)
    solve_upper = jnp.where(positions == count - 2, 0.0, upper_inner)
    from_prev = jnp.where(positions == 0, -first_lower, 0.0)
    from_next = jnp.where(positions == count - 2, -last_upper, 0.0)
    inner_rights = take_rows(rights, 0, count - 1, axis_index)
    local_part, prev_part, next_part = cyclic(
        solve_lower, diagonal, solve_upper, (inner_rights, from_prev, from_next), axis_index
    )
    heads = (
        take_rows(local_part, 0, 1, axis_index),
        take_rows(prev_part, 0, 1, axis_index),
        take_rows(next_part, 0, 1, axis_index),
    )
    head_local, head_prev, head_next, last_coupling = fetch_next(heads)
    tail_local = take_rows(local_part, count - 2, count - 1, axis_index)
    tail_prev = take_rows(prev_part, count - 2, count - 1, axis_index)
    tail_next = take_rows(next_part, count - 2, count - 1, axis_index)
    lower_last = take_rows(lower_band, count - 1, count, axis_index)
    right_last = take_rows(rights, count - 1, count, axis_index)
    coeff_lower = lower_last * tail_prev
    coeff_diag = (
        1.0 - lower_last - last_coupling + lower_last * tail_next + last_coupling * head_prev
    )
    coeff_upper = last_coupling * head_next
    coeff_right = right_last - lower_last * tail_local - last_coupling * head_local
    interface_value = reduced(coeff_lower, coeff_diag, coeff_upper, coeff_right)
    previous = fetch_prev(interface_value)
    inner_values = local_part + prev_part * previous + next_part * interface_value
    return jnp.concatenate([inner_values, interface_value], axis=axis_index)


def on_device(thermal_state, sideways_face_flux_factor, downward_face_flux_factor):
    sideways_node_count = thermal_state.shape[2]
    grouped_sweep_rows = jnp.stack([thermal_state, sideways_face_flux_factor])
    padded = extended(grouped_sweep_rows, (("lat", 3),), 1)
    initial_operand_swapped = padded[0, :, :, :sideways_node_count]
    source_vector_swapped = padded[0, :, :, 2:]
    source_vector_downward = padded[1, :, :, 2:]
    known_operator_term = thermal_state + sideways_coupling_quotient * (
        source_vector_downward * (source_vector_swapped - thermal_state)
        - sideways_face_flux_factor * (thermal_state - initial_operand_swapped)
    )

    def depth_next(heads):
        arrived = from_behind(
            (heads[0], heads[1], heads[2], downward_face_flux_factor[0:1]), "depth", -1
        )
        return (arrived[0], arrived[1], arrived[2], -ratio_z * arrived[3])

    def depth_reduced(coeff_lower, coeff_diag, coeff_upper, coeff_right):
        gathered = (
            lax.all_gather(coeff_lower, "depth", axis=0, tiled=True),
            lax.all_gather(coeff_diag, "depth", axis=0, tiled=True),
            lax.all_gather(coeff_upper, "depth", axis=0, tiled=True),
            lax.all_gather(coeff_right, "depth", axis=0, tiled=True),
        )
        solved = cyclic(gathered[0], gathered[1], gathered[2], (gathered[3],), 0)[0]
        return lax.dynamic_slice_in_dim(solved, lax.axis_index("depth"), 1, 0)

    def depth_prev(interface_value):
        return from_behind(interface_value, "depth", 1)

    half_step = partition_solve(
        -ratio_z * downward_face_flux_factor,
        -ratio_z * downward_face_flux_factor[1:],
        known_operator_term,
        0,
        depth_next,
        depth_reduced,
        depth_prev,
    )
    reflected = 2.0 * half_step - known_operator_term
    lines = lax.all_to_all(reflected, "lat", split_axis=0, concat_axis=2, tiled=True)
    conduct_lines = lax.all_to_all(
        sideways_face_flux_factor, "lat", split_axis=0, concat_axis=2, tiled=True
    )
    lower_band = -sideways_coupling_quotient * conduct_lines
    upper_band = -sideways_coupling_quotient * jnp.concatenate(
        [conduct_lines[:, :, 1:], jnp.zeros_like(conduct_lines[:, :, :1])], axis=2
    )
    diagonal = 1.0 - lower_band - upper_band
    solve_lower = jnp.concatenate(
        [jnp.zeros_like(lower_band[:, :, :1]), lower_band[:, :, 1:]], axis=2
    )
    solved = cyclic(solve_lower, diagonal, upper_band, (lines,), 2)[0]
    return lax.all_to_all(solved, "lat", split_axis=2, concat_axis=0, tiled=True)


def solution(mesh):
    in_specs = (P("depth", None, "lat"), P("depth", None, "lat"), P("depth", None, "lat"))
    out_specs = P("depth", None, "lat")
    return jax.shard_map(
        on_device, mesh=mesh, in_specs=in_specs, out_specs=out_specs, check_vma=False
    )
```

profile of v0, /device:TPU:1, one launch (start us, length us, event | category | flops | bytes accessed | tf_op | source)
XLA Modules:
  0.0 245.1 jit_solution(14447107847641421287)
XLA Ops:
  0.0 1.3 slice_maximum_fusion
  1.3 8.8 %collective-permute-start = (f32[2,32,8,1]{3,2,1,0:T(8,128)S(1)}, f32[2,32,8,1]{3,2,1,0:T(8,128)S(1)}, u32[]{:S(2)}, u32[]{:S(2)}) collective-permute-start(f32[2,32,8,1]{3,2,1,0:T(8,128)S(1)} %get-tuple-element.67), channel_id=1, source_target_pairs={{1,0},{2,1},{3,2},{4,3},{5,4},{6,5},{7,6},{8,7},{9,8},{10,9},{11,1... | collective-permute-start | bytes 6152 | tf_op jit(solution)/shard_map/ppermute | solution.py:18
  10.1 1.9 collective-permute-start.1
  12.0 0.7 slice.672
  12.7 1.3 collective-permute-start.2
  14.0 0.9 broadcast_multiply_fusion.1
  14.9 0.9 slice_multiply_fusion
  15.9 1.2 fusion.5
  18.8 1.3 collective-permute-start.3
  20.3 1.3 collective-permute-start.4
  21.6 2.2 collective-permute-done.3
  23.8 2.1 collective-permute-done.4
  25.9 1.3 collective-permute-start.5
  27.2 34.0 %all_gather.13 = f32[32,8,128]{2,1,0:T(8,128)S(1)} all-gather(f32[1,8,128]{2,1,0:T(8,128)S(1)} %get-tuple-element.205), channel_id=1, replica_groups=mesh['depth'=32,'lat'=16] {'depth'}, dimensions={0}, use_global_device_ids=true | all-gather | bytes 135168 | tf_op jit(solution)/shard_map/all_gather | solution.py:141
  61.2 28.5 %all_gather.14 = f32[32,8,128]{2,1,0:T(8,128)S(1)} all-gather(f32[1,8,128]{2,1,0:T(8,128)S(1)} %get-tuple-element.84), channel_id=1, replica_groups=mesh['depth'=32,'lat'=16] {'depth'}, dimensions={0}, use_global_device_ids=true | all-gather | bytes 135168 | tf_op jit(solution)/shard_map/all_gather | solution.py:142
  89.7 28.7 %all_gather.12 = f32[32,8,128]{2,1,0:T(8,128)S(1)} all-gather(f32[1,8,128]{2,1,0:T(8,128)S(1)} %get-tuple-element.85), channel_id=1, replica_groups=mesh['depth'=32,'lat'=16] {'depth'}, dimensions={0}, use_global_device_ids=true | all-gather | bytes 135168 | tf_op jit(solution)/shard_map/all_gather | solution.py:144
  118.4 29.4 %all_gather.15 = f32[32,8,128]{2,1,0:T(8,128)S(1)} all-gather(f32[1,8,128]{2,1,0:T(8,128)S(1)} %multiply_multiply_fusion), channel_id=1, replica_groups=mesh['depth'=32,'lat'=16] {'depth'}, dimensions={0}, use_global_device_ids=true | all-gather | bytes 135168 | tf_op jit(solution)/shard_map/all_gather | solution.py:143
  148.9 1.7 collective-permute-start.6
  150.6 44.6 %all-to-all-start.1 = ((f32[32,8,128]{2,1,0:T(8,128)}), f32[32,8,128]{2,1,0:T(8,128)S(1)}, u32[]{:S(2)}, u32[]{:S(2)}) async-start(f32[32,8,128]{2,1,0:T(8,128)} %param.4), calls=%async_computation.1 | async-start | bytes 262144 | tf_op jit(solution)/shard_map/all_to_all | solution.py:163
  195.3 0.7 fusion.9
  195.9 8.5 %all-to-all-done.1 = f32[32,8,128]{2,1,0:T(8,128)S(1)} async-done(((f32[32,8,128]{2,1,0:T(8,128)}), f32[32,8,128]{2,1,0:T(8,128)S(1)}, u32[]{:S(2)}, u32[]{:S(2)}) %all-to-all-start.1) | async-done | bytes 131104 | tf_op jit(solution)/shard_map/all_to_all | solution.py:163
  204.4 3.6 %all-to-all-start = ((f32[32,8,128]{2,1,0:T(8,128)}), f32[32,8,128]{2,1,0:T(8,128)S(1)}, u32[]{:S(2)}, u32[]{:S(2)}) async-start(f32[32,8,128]{2,1,0:T(8,128)} %fusion.9), calls=%async_computation | async-start | bytes 262144 | tf_op jit(solution)/shard_map/all_to_all | solution.py:162
  208.6 7.8 %all-to-all-done = f32[32,8,128]{2,1,0:T(8,128)S(1)} async-done(((f32[32,8,128]{2,1,0:T(8,128)}), f32[32,8,128]{2,1,0:T(8,128)S(1)}, u32[]{:S(2)}, u32[]{:S(2)}) %all-to-all-start) | async-done | bytes 131104 | tf_op jit(solution)/shard_map/all_to_all | solution.py:162
  217.0 0.2 multiply_add_fusion.17
  217.8 0.2 multiply_add_fusion.15
  222.4 1.0 copy.11
  223.4 3.3 %reshape = f32[16,1,2048]{2,1,0:T(1,128)S(1)} reshape(f32[2048,2,8]{2,1,0:T(2,128)S(1)} %bitcast.51) | data formatting | bytes 262144
  226.8 11.8 %all_to_all.54 = f32[16,1,2048]{2,1,0:T(1,128)S(1)} all-to-all(f32[16,1,2048]{2,1,0:T(1,128)S(1)} %reshape), channel_id=1, replica_groups=mesh['depth'=32,'lat'=16] {'lat'}, dimensions={0} | all-to-all | bytes 262144 | tf_op jit(solution)/shard_map/all_to_all | solution.py:175
  238.6 0.5 broadcast.435
  239.1 0.9 reduce
  240.1 3.2 %reshape.1 = f32[2048,2,8]{2,1,0:T(2,128)S(1)} reshape(f32[16,2048]{1,0:T(8,128)S(1)} %reduce) | data formatting | bytes 262144
  243.2 1.9 copy.15
  (152 shorter events, 8.2 us)
Async XLA Ops:
  0.0 15.9 %copy-start = (f32[32,8,128]{2,1,0:T(8,128)S(1)}, f32[32,8,128]{2,1,0:T(8,128)}, u32[]{:S(2)}) copy-start(f32[32,8,128]{2,1,0:T(8,128)} %param.3) | copy-start | bytes 393220
  0.0 17.2 %copy-start.1 = (f32[32,8,128]{2,1,0:T(8,128)S(1)}, f32[32,8,128]{2,1,0:T(8,128)}, u32[]{:S(2)}) copy-start(f32[32,8,128]{2,1,0:T(8,128)} %param.5) | copy-start | bytes 393220
  1.3 14.6 %collective-permute-start = (f32[2,32,8,1]{3,2,1,0:T(8,128)S(1)}, f32[2,32,8,1]{3,2,1,0:T(8,128)S(1)}, u32[]{:S(2)}, u32[]{:S(2)}) collective-permute-start(f32[2,32,8,1]{3,2,1,0:T(8,128)S(1)} %get-tuple-element.67), channel_id=1, source_target_pairs={{1,0},{2,1},{3,2},{4,3},{5,4},{6,5},{7,6},{8,7},{9,8},{10,9},{11,1... | collective-permute-start | bytes 6152 | tf_op jit(solution)/shard_map/ppermute | solution.py:18
  10.1 5.8 %collective-permute-start.1 = (f32[2,32,8,1]{3,2,1,0:T(8,128)S(1)}, f32[2,32,8,1]{3,2,1,0:T(8,128)S(1)}, u32[]{:S(2)}, u32[]{:S(2)}) collective-permute-start(f32[2,32,8,1]{3,2,1,0:T(8,128)S(1)} %get-tuple-element.68), channel_id=1, source_target_pairs={{0,1},{1,2},{2,3},{3,4},{4,5},{5,6},{6,7},{7,8},{8,9},{9,10},{10,1... | collective-permute-start | bytes 6152 | tf_op jit(solution)/shard_map/ppermute | solution.py:17
  12.7 8.9 %collective-permute-start.2 = (f32[1,8,128]{2,1,0:T(8,128)S(1)}, f32[1,8,128]{2,1,0:T(8,128)S(1)}, u32[]{:S(2)}, u32[]{:S(2)}) collective-permute-start(f32[1,8,128]{2,1,0:T(8,128)S(1)} %slice.672), channel_id=1, source_target_pairs={{16,0},{32,16},{48,32},{64,48},{80,64},{96,80},{112,96},{128,112},... | collective-permute-start | bytes 12296 | tf_op jit(solution)/shard_map/ppermute | solution.py:26
  18.8 5.0 %collective-permute-start.3 = (f32[1,8,128]{2,1,0:T(8,128)S(1)}, f32[1,8,128]{2,1,0:T(8,128)S(1)}, u32[]{:S(2)}, u32[]{:S(2)}) collective-permute-start(f32[1,8,128]{2,1,0:T(8,128)S(1)} %slice.870), channel_id=1, source_target_pairs={{16,0},{32,16},{48,32},{64,48},{80,64},{96,80},{112,96},{128,112},... | collective-permute-start | bytes 12296 | tf_op jit(solution)/shard_map/ppermute | solution.py:26
  20.3 5.6 %collective-permute-start.4 = (f32[1,8,128]{2,1,0:T(8,128)S(1)}, f32[1,8,128]{2,1,0:T(8,128)S(1)}, u32[]{:S(2)}, u32[]{:S(2)}) collective-permute-start(f32[1,8,128]{2,1,0:T(8,128)S(1)} %slice.884), channel_id=1, source_target_pairs={{16,0},{32,16},{48,32},{64,48},{80,64},{96,80},{112,96},{128,112},... | collective-permute-start | bytes 12296 | tf_op jit(solution)/shard_map/ppermute | solution.py:26
  25.9 92.6 %collective-permute-start.5 = (f32[1,8,128]{2,1,0:T(8,128)S(1)}, f32[1,8,128]{2,1,0:T(8,128)S(1)}, u32[]{:S(2)}, u32[]{:S(2)}) collective-permute-start(f32[1,8,128]{2,1,0:T(8,128)S(1)} %get-tuple-element.212), channel_id=1, source_target_pairs={{16,0},{32,16},{48,32},{64,48},{80,64},{96,80},{112,96},{128,112},... | collective-permute-start | bytes 12296 | tf_op jit(solution)/shard_map/ppermute | solution.py:26
  148.9 46.3 %collective-permute-start.6 = (f32[1,8,128]{2,1,0:T(8,128)S(1)}, f32[1,8,128]{2,1,0:T(8,128)S(1)}, u32[]{:S(2)}, u32[]{:S(2)}) collective-permute-start(f32[1,8,128]{2,1,0:T(8,128)S(1)} %fusion.18), channel_id=1, source_target_pairs={{0,16},{16,32},{32,48},{48,64},{64,80},{80,96},{96,112},{112,128},... | collective-permute-start | bytes 12296 | tf_op jit(solution)/shard_map/ppermute | solution.py:26
  150.6 53.8 %all-to-all-start.1 = ((f32[32,8,128]{2,1,0:T(8,128)}), f32[32,8,128]{2,1,0:T(8,128)S(1)}, u32[]{:S(2)}, u32[]{:S(2)}) async-start(f32[32,8,128]{2,1,0:T(8,128)} %param.4), calls=%async_computation.1 | async-start | bytes 262144 | tf_op jit(solution)/shard_map/all_to_all | solution.py:163
  204.4 12.0 %all-to-all-start = ((f32[32,8,128]{2,1,0:T(8,128)}), f32[32,8,128]{2,1,0:T(8,128)S(1)}, u32[]{:S(2)}, u32[]{:S(2)}) async-start(f32[32,8,128]{2,1,0:T(8,128)} %fusion.9), calls=%async_computation | async-start | bytes 262144 | tf_op jit(solution)/shard_map/all_to_all | solution.py:162
where the time goes:
time: 246 us; the launch traced here: 245 us
  blocking collectives  132 us (54%)
  starting transfers between devices  65.8 us (27%)
  waiting for transfers between devices  20.6 us (8%)
  local copies, waits for them, and re-layouts  14.5 us (6%)
  other arithmetic  10.7 us (4%)
    all_to_all x1, starting transfers between devices, on_device(): lax.all_to_all(sideways_face_flux_factor, 'lat', split_axis=0, concat_axi...  44.6 us
    all_gather x1, blocking collectives, depth_reduced(): lax.all_gather(coeff_lower, 'depth', axis=0, tiled=True)  34 us
    all_gather x1, blocking collectives, depth_reduced(): lax.all_gather(coeff_upper, 'depth', axis=0, tiled=True)  29.4 us
    all_gather x1, blocking collectives, depth_reduced(): lax.all_gather(coeff_right, 'depth', axis=0, tiled=True)  28.7 us
    all_gather x1, blocking collectives, depth_reduced(): lax.all_gather(coeff_diag, 'depth', axis=0, tiled=True)  28.5 us
    all_to_all x1, blocking collectives, on_device(): lax.all_to_all(solved, 'lat', split_axis=2, concat_axis=0, tiled=True)  11.8 us
    ppermute x1, starting transfers between devices, extended(): after = lax.ppermute(first, axis, down)  8.79 us
    all_to_all x1, waiting for transfers between devices, on_device(): lax.all_to_all(sideways_face_flux_factor, 'lat', split_axis=0, concat_axi...  8.46 us
  transfers between devices with their start and end apart: 9, of which 4 were waited for; matrix products, arithmetic and copies ran while one was open for 3% of the time, Pallas kernels for 0%

commit v1 on v0

--- a/solution.py
+++ b/solution.py
@@ -5,6 +5,15 @@
 
 sideways_coupling_quotient = 20.0
 ratio_z = 2000.0
+
+
+def shape_block(slab_in):
+    v_next = lax.axis_size("lat")
+    current_arr = jnp.split(slab_in, v_next, 2)
+    tall = jnp.stack(current_arr, axis=0)
+    y = lax.all_to_all(tall, "lat", 0, 0)
+    block_now = jnp.concatenate(y, 0)
+    return block_now
 
 
 def extended(x, sides, width):
@@ -172,7 +181,7 @@
         [jnp.zeros_like(lower_band[:, :, :1]), lower_band[:, :, 1:]], axis=2
     )
     solved = cyclic(solve_lower, diagonal, upper_band, (lines,), 2)[0]
-    return lax.all_to_all(solved, "lat", split_axis=2, concat_axis=0, tiled=True)
+    return shape_block(solved)
 
 
 def solution(mesh):

time: 246 us -> 236 us (0.959)
  local copies, waits for them, and re-layouts: 14.5 us -> 4.56 us
  other arithmetic: 10.7 us -> 7.98 us
    unnamed x6 -> x20, local copies, waits for them, and re-layouts: 6.5 us -> 0.72 us
  transfers between devices with their start and end apart: 9 -> 9, of which waited for: 4 -> 5; matrix products, arithmetic and copies ran while one was open for 3% -> 2% of each run, Pallas kernels for 0% -> 0%
where the time goes in v1:
time: 236 us; the launch traced here: 235 us
  blocking collectives  132 us (56%)
  starting transfers between devices  67.2 us (28%)
  waiting for transfers between devices  21.9 us (9%)
  other arithmetic  7.98 us (3%)
  local copies, waits for them, and re-layouts  4.56 us (2%)
    all_to_all x1, starting transfers between devices, on_device(): lax.all_to_all(sideways_face_flux_factor, 'lat', split_axis=0, concat_axi...  46.2 us
    all_gather x1, blocking collectives, depth_reduced(): lax.all_gather(coeff_lower, 'depth', axis=0, tiled=True)  33.7 us
    all_gather x1, blocking collectives, depth_reduced(): lax.all_gather(coeff_upper, 'depth', axis=0, tiled=True)  29.3 us
    all_gather x1, blocking collectives, depth_reduced(): lax.all_gather(coeff_right, 'depth', axis=0, tiled=True)  28.8 us
    all_gather x1, blocking collectives, depth_reduced(): lax.all_gather(coeff_diag, 'depth', axis=0, tiled=True)  28.4 us
    all_to_all x1, blocking collectives, shape_block(): y = lax.all_to_all(tall, 'lat', 0, 0)  11.9 us
    ppermute x1, starting transfers between devices, extended(): after = lax.ppermute(first, axis, down)  8.79 us
    all_to_all x1, waiting for transfers between devices, on_device(): lax.all_to_all(sideways_face_flux_factor, 'lat', split_axis=0, concat_axi...  8.46 us
  transfers between devices with their start and end apart: 9, of which 5 were waited for; matrix products, arithmetic and copies ran while one was open for 2% of the time, Pallas kernels for 0%

profile of v1, /device:TPU:1, one launch (start us, length us, event | category | flops | bytes accessed | tf_op | source)
XLA Modules:
  0.0 235.0 jit_solution(7500737944736265945)
XLA Ops:
  0.0 1.3 slice_maximum_fusion
  1.3 8.8 %collective-permute-start = (f32[2,32,8,1]{3,2,1,0:T(8,128)S(1)}, f32[2,32,8,1]{3,2,1,0:T(8,128)S(1)}, u32[]{:S(2)}, u32[]{:S(2)}) collective-permute-start(f32[2,32,8,1]{3,2,1,0:T(8,128)S(1)} %get-tuple-element.67), channel_id=1, source_target_pairs={{1,0},{2,1},{3,2},{4,3},{5,4},{6,5},{7,6},{8,7},{9,8},{10,9},{11,1... | collective-permute-start | bytes 6152 | tf_op jit(solution)/shard_map/ppermute | solution.py:27
  10.1 1.9 collective-permute-start.1
  12.0 1.3 collective-permute-start.2
  13.5 1.8 collective-permute-done.1
  15.3 1.2 fusion.5
  16.9 0.2 multiply_add_fusion.43
  17.3 0.2 multiply_add_fusion.41
  18.1 1.3 collective-permute-start.3
  19.6 1.3 collective-permute-start.4
  20.9 1.6 collective-permute-done.3
  22.5 2.1 collective-permute-done.4
  24.6 1.3 collective-permute-start.5
  25.9 33.7 %all_gather.13 = f32[32,8,128]{2,1,0:T(8,128)S(1)} all-gather(f32[1,8,128]{2,1,0:T(8,128)S(1)} %get-tuple-element.205), channel_id=1, replica_groups=mesh['depth'=32,'lat'=16] {'depth'}, dimensions={0}, use_global_device_ids=true | all-gather | bytes 135168 | tf_op jit(solution)/shard_map/all_gather | solution.py:150
  59.6 28.4 %all_gather.14 = f32[32,8,128]{2,1,0:T(8,128)S(1)} all-gather(f32[1,8,128]{2,1,0:T(8,128)S(1)} %get-tuple-element.84), channel_id=1, replica_groups=mesh['depth'=32,'lat'=16] {'depth'}, dimensions={0}, use_global_device_ids=true | all-gather | bytes 135168 | tf_op jit(solution)/shard_map/all_gather | solution.py:151
  88.1 28.8 %all_gather.12 = f32[32,8,128]{2,1,0:T(8,128)S(1)} all-gather(f32[1,8,128]{2,1,0:T(8,128)S(1)} %get-tuple-element.85), channel_id=1, replica_groups=mesh['depth'=32,'lat'=16] {'depth'}, dimensions={0}, use_global_device_ids=true | all-gather | bytes 135168 | tf_op jit(solution)/shard_map/all_gather | solution.py:153
  116.9 29.3 %all_gather.15 = f32[32,8,128]{2,1,0:T(8,128)S(1)} all-gather(f32[1,8,128]{2,1,0:T(8,128)S(1)} %multiply_multiply_fusion), channel_id=1, replica_groups=mesh['depth'=32,'lat'=16] {'depth'}, dimensions={0}, use_global_device_ids=true | all-gather | bytes 135168 | tf_op jit(solution)/shard_map/all_gather | solution.py:152
  147.3 1.7 collective-permute-start.6
  149.0 46.2 %all-to-all-start.1 = ((f32[32,8,128]{2,1,0:T(8,128)}), f32[32,8,128]{2,1,0:T(8,128)S(1)}, u32[]{:S(2)}, u32[]{:S(2)}) async-start(f32[32,8,128]{2,1,0:T(8,128)} %param.4), calls=%async_computation.1 | async-start | bytes 262144 | tf_op jit(solution)/shard_map/all_to_all | solution.py:172
  195.2 0.7 fusion.9
  195.9 8.5 %all-to-all-done.1 = f32[32,8,128]{2,1,0:T(8,128)S(1)} async-done(((f32[32,8,128]{2,1,0:T(8,128)}), f32[32,8,128]{2,1,0:T(8,128)S(1)}, u32[]{:S(2)}, u32[]{:S(2)}) %all-to-all-start.1) | async-done | bytes 131104 | tf_op jit(solution)/shard_map/all_to_all | solution.py:172
  204.4 3.4 %all-to-all-start = ((f32[32,8,128]{2,1,0:T(8,128)}), f32[32,8,128]{2,1,0:T(8,128)S(1)}, u32[]{:S(2)}, u32[]{:S(2)}) async-start(f32[32,8,128]{2,1,0:T(8,128)} %fusion.9), calls=%async_computation | async-start | bytes 262144 | tf_op jit(solution)/shard_map/all_to_all | solution.py:171
  208.3 8.0 %all-to-all-done = f32[32,8,128]{2,1,0:T(8,128)S(1)} async-done(((f32[32,8,128]{2,1,0:T(8,128)}), f32[32,8,128]{2,1,0:T(8,128)S(1)}, u32[]{:S(2)}, u32[]{:S(2)}) %all-to-all-start) | async-done | bytes 131104 | tf_op jit(solution)/shard_map/all_to_all | solution.py:171
  216.4 0.2 multiply_add_fusion.18
  216.9 0.2 multiply_add_fusion.17
  217.7 0.2 multiply_add_fusion.15
  218.4 0.2 multiply_add_fusion.13
  219.2 0.2 multiply_add_fusion.11
  220.0 0.2 multiply_add_fusion.9
  220.8 0.2 multiply_add_fusion.7
  222.5 11.9 %all_to_all.41 = f32[16,2,8,128]{3,2,1,0:T(8,128)S(1)} all-to-all(f32[16,2,8,128]{3,2,1,0:T(8,128)S(1)} %constant_dynamic-update-slice_fusion), channel_id=1, replica_groups=mesh['depth'=32,'lat'=16] {'lat'}, dimensions={0} | all-to-all | bytes 262144 | tf_op jit(solution)/shard_map/all_to_all | solution.py:14
  234.4 0.7 copy.33
  (162 shorter events, 6.9 us)
Async XLA Ops:
  0.0 12.0 %copy-start.1 = (f32[32,8,128]{2,1,0:T(8,128)S(1)}, f32[32,8,128]{2,1,0:T(8,128)}, u32[]{:S(2)}) copy-start(f32[32,8,128]{2,1,0:T(8,128)} %param.5) | copy-start | bytes 393220
  1.3 12.2 %collective-permute-start = (f32[2,32,8,1]{3,2,1,0:T(8,128)S(1)}, f32[2,32,8,1]{3,2,1,0:T(8,128)S(1)}, u32[]{:S(2)}, u32[]{:S(2)}) collective-permute-start(f32[2,32,8,1]{3,2,1,0:T(8,128)S(1)} %get-tuple-element.67), channel_id=1, source_target_pairs={{1,0},{2,1},{3,2},{4,3},{5,4},{6,5},{7,6},{8,7},{9,8},{10,9},{11,1... | collective-permute-start | bytes 6152 | tf_op jit(solution)/shard_map/ppermute | solution.py:27
  10.1 5.2 %collective-permute-start.1 = (f32[2,32,8,1]{3,2,1,0:T(8,128)S(1)}, f32[2,32,8,1]{3,2,1,0:T(8,128)S(1)}, u32[]{:S(2)}, u32[]{:S(2)}) collective-permute-start(f32[2,32,8,1]{3,2,1,0:T(8,128)S(1)} %get-tuple-element.68), channel_id=1, source_target_pairs={{0,1},{1,2},{2,3},{3,4},{4,5},{5,6},{6,7},{7,8},{8,9},{9,10},{10,1... | collective-permute-start | bytes 6152 | tf_op jit(solution)/shard_map/ppermute | solution.py:26
  12.0 8.9 %collective-permute-start.2 = (f32[1,8,128]{2,1,0:T(8,128)S(1)}, f32[1,8,128]{2,1,0:T(8,128)S(1)}, u32[]{:S(2)}, u32[]{:S(2)}) collective-permute-start(f32[1,8,128]{2,1,0:T(8,128)S(1)} %slice.672), channel_id=1, source_target_pairs={{16,0},{32,16},{48,32},{64,48},{80,64},{96,80},{112,96},{128,112},... | collective-permute-start | bytes 12296 | tf_op jit(solution)/shard_map/ppermute | solution.py:35
  13.4 1.9 copy-start
  18.1 4.4 %collective-permute-start.3 = (f32[1,8,128]{2,1,0:T(8,128)S(1)}, f32[1,8,128]{2,1,0:T(8,128)S(1)}, u32[]{:S(2)}, u32[]{:S(2)}) collective-permute-start(f32[1,8,128]{2,1,0:T(8,128)S(1)} %slice.870), channel_id=1, source_target_pairs={{16,0},{32,16},{48,32},{64,48},{80,64},{96,80},{112,96},{128,112},... | collective-permute-start | bytes 12296 | tf_op jit(solution)/shard_map/ppermute | solution.py:35
  19.6 5.0 %collective-permute-start.4 = (f32[1,8,128]{2,1,0:T(8,128)S(1)}, f32[1,8,128]{2,1,0:T(8,128)S(1)}, u32[]{:S(2)}, u32[]{:S(2)}) collective-permute-start(f32[1,8,128]{2,1,0:T(8,128)S(1)} %slice.884), channel_id=1, source_target_pairs={{16,0},{32,16},{48,32},{64,48},{80,64},{96,80},{112,96},{128,112},... | collective-permute-start | bytes 12296 | tf_op jit(solution)/shard_map/ppermute | solution.py:35
  24.6 92.3 %collective-permute-start.5 = (f32[1,8,128]{2,1,0:T(8,128)S(1)}, f32[1,8,128]{2,1,0:T(8,128)S(1)}, u32[]{:S(2)}, u32[]{:S(2)}) collective-permute-start(f32[1,8,128]{2,1,0:T(8,128)S(1)} %get-tuple-element.212), channel_id=1, source_target_pairs={{16,0},{32,16},{48,32},{64,48},{80,64},{96,80},{112,96},{128,112},... | collective-permute-start | bytes 12296 | tf_op jit(solution)/shard_map/ppermute | solution.py:35
  147.3 47.9 %collective-permute-start.6 = (f32[1,8,128]{2,1,0:T(8,128)S(1)}, f32[1,8,128]{2,1,0:T(8,128)S(1)}, u32[]{:S(2)}, u32[]{:S(2)}) collective-permute-start(f32[1,8,128]{2,1,0:T(8,128)S(1)} %fusion.18), channel_id=1, source_target_pairs={{0,16},{16,32},{32,48},{48,64},{64,80},{80,96},{96,112},{112,128},... | collective-permute-start | bytes 12296 | tf_op jit(solution)/shard_map/ppermute | solution.py:35
  149.0 55.4 %all-to-all-start.1 = ((f32[32,8,128]{2,1,0:T(8,128)}), f32[32,8,128]{2,1,0:T(8,128)S(1)}, u32[]{:S(2)}, u32[]{:S(2)}) async-start(f32[32,8,128]{2,1,0:T(8,128)} %param.4), calls=%async_computation.1 | async-start | bytes 262144 | tf_op jit(solution)/shard_map/all_to_all | solution.py:172
  204.4 11.9 %all-to-all-start = ((f32[32,8,128]{2,1,0:T(8,128)}), f32[32,8,128]{2,1,0:T(8,128)S(1)}, u32[]{:S(2)}, u32[]{:S(2)}) async-start(f32[32,8,128]{2,1,0:T(8,128)} %fusion.9), calls=%async_computation | async-start | bytes 262144 | tf_op jit(solution)/shard_map/all_to_all | solution.py:171
